TPU v7x, 512 devices: a whole 4x8x8 slice. The times are simulated.
512 devices in a mesh: req: 64 (over z, x, core), tp: 8 (over y).
Axes of the slice: x: 4, y: 8, z: 8, core: 2. Of those that a mesh axis runs over, the one named last changes fastest.
Arguments:
- q_new: bfloat16 [4096, 5120], P('req', 'tp'), may hold values from -6 to 6
- k_new: bfloat16 [4096, 1024], P('req', 'tp'), may hold values from -15 to 15
- v_new: bfloat16 [4096, 1024], P('req', 'tp'), may hold values from -6 to 6
- k_cache: bfloat16 [1024, 128, 1024], P('req', None, 'tp'), may hold values from -16 to 16
- v_cache: bfloat16 [1024, 128, 1024], P('req', None, 'tp'), may hold values from -6 to 6
- lengths: int32 [32], replicated, may hold values from 1 to 4096, as said below
- page_table: int32 [32, 32], replicated, may hold values from -1 to 1023, as said below
- w_out: bfloat16 [5120, 5120], P('req', 'tp'), may hold values from -0.078125 to 0.078125
Outputs:
- attn_out: bfloat16 [4096, 5120], P('req')
Inputs may be any that keep to these rules, and one draw needn't show every extreme that they name: `lengths`: the last request, 31, has exactly 4096 cached tokens; every request has at least one. `page_table`: request r uses ceil(lengths[r] / 128) logical pages. Its first ceil(ceil(lengths[r] / 128) / 2) logical pages lie among global pages 2r * 16 to (2r + 1) * 16 - 1, the rest among (2r + 1) * 16 to (2r + 2) * 16 - 1; distinct logical pages use distinct global pages; entries past a request's last page are -1.
All inputs are finite; a program needn't handle non-finite values.
Results may differ from a plain program's by a relative error of at most 0.024.
Values may be sent and summed in bfloat16 or wider, within the bound.
No kernel may reach another device: no remote copies, remote signals or barrier semaphores. Data moves between devices by JAX's collectives and lax.ppermute only.
A program may use at most 64 MiB of HBM per device.

v0:
```python
import math
import jax
import jax.numpy as jnp
from jax import lax
from jax.sharding import PartitionSpec as P

HD = 128
GROUP = 5
BLOCK_PAGES = 4
ROPE_BASE = 1000000.0
FLOOR_SCORE = -1e30


def from_partner(value, axis, distance):
    return lax.ppermute(value, axis, [(i, i ^ 1 << distance) for i in range(lax.axis_size(axis))])


def rotate(values, places):
    inverse = 1.0 / ROPE_BASE ** (jnp.arange(0, HD, 2).astype(jnp.float32) / HD)
    angles = places.astype(jnp.float32)[:, None] * inverse[None, :]
    cosine = jnp.concatenate([jnp.cos(angles), jnp.cos(angles)], axis=-1)[:, None, :]
    sine = jnp.concatenate([jnp.sin(angles), jnp.sin(angles)], axis=-1)[:, None, :]
    first_half = values[..., : HD // 2]
    second_half = values[..., HD // 2 :]
    turned = jnp.concatenate([-second_half, first_half], axis=-1)
    return values * cosine + turned * sine


def absorb(state, queries, block_keys, block_values, allowed, scale):
    running_max, running_sum, output = state
    scores = (
        jnp.einsum("qcgd,kcd->cgqk", queries, block_keys, preferred_element_type=jnp.float32)
        * scale
    )
    scores = jnp.where(allowed[None, None], scores, FLOOR_SCORE)
    new_max = jnp.maximum(running_max, jnp.max(scores, axis=-1))
    factor = jnp.exp(running_max - new_max)
    weights = jnp.where(allowed[None, None], jnp.exp(scores - new_max[..., None]), 0.0)
    running_sum = running_sum * factor + jnp.sum(weights, axis=-1)
    mixed = jnp.einsum(
        "cgqk,kcd->qcgd",
        weights.astype(jnp.bfloat16),
        block_values,
        preferred_element_type=jnp.float32,
    )
    output = output * jnp.transpose(factor, (2, 0, 1))[..., None] + mixed
    return (new_max, running_sum, output)


def tensor_total(partial_value):
    return lax.psum(partial_value.astype(jnp.bfloat16), "tp")


def shards(q_new, k_new, v_new, k_cache, v_cache, lengths, page_table, w_out):
    own_rows = q_new.shape[0]
    all_rows = 2 * own_rows
    local_heads = k_new.shape[1] // HD
    pages_local = k_cache.shape[0]
    page_rows = k_cache.shape[1]
    block_rows = BLOCK_PAGES * page_rows
    scale = 1.0 / math.sqrt(HD)
    device_row = lax.axis_index("req")
    parity = device_row % 2
    request = device_row // 2
    length = lengths[request]
    own_places = length + parity * own_rows + jnp.arange(own_rows)
    own_queries = rotate(
        q_new.reshape(own_rows, local_heads * GROUP, HD).astype(jnp.float32), own_places
    ).astype(jnp.bfloat16)
    own_keys = rotate(
        k_new.reshape(own_rows, local_heads, HD).astype(jnp.float32), own_places
    ).astype(jnp.bfloat16)
    own_values = v_new.reshape(own_rows, local_heads, HD)
    peer_queries, peer_keys, peer_values = from_partner(
        (own_queries, own_keys, own_values), "req", 0
    )

    def ordered(mine, theirs):
        return jnp.where(
            parity == 0,
            jnp.concatenate([mine, theirs], axis=0),
            jnp.concatenate([theirs, mine], axis=0),
        )

    queries = ordered(own_queries, peer_queries).reshape(all_rows, local_heads, GROUP, HD)
    fresh_keys = ordered(own_keys, peer_keys)
    fresh_values = ordered(own_values, peer_values)
    state = (
        jnp.full((local_heads, GROUP, all_rows), FLOOR_SCORE, jnp.float32),
        jnp.zeros((local_heads, GROUP, all_rows), jnp.float32),
        jnp.zeros((all_rows, local_heads, GROUP, HD), jnp.float32),
    )
    token_index = jnp.arange(all_rows)
    causal = (token_index[None, :] <= token_index[:, None]) & (parity == 1)
    state = absorb(state, queries, fresh_keys, fresh_values, causal, scale)
    page_count = (length + page_rows - 1) // page_rows
    even_pages = (page_count + 1) // 2
    first_page = jnp.where(parity == 0, 0, even_pages)
    last_page = jnp.where(parity == 0, even_pages, page_count)
    table_row = jnp.concatenate([page_table[request], jnp.full((BLOCK_PAGES,), -1, jnp.int32)])
    offset = device_row * pages_local
    block_count = (last_page - first_page + BLOCK_PAGES - 1) // BLOCK_PAGES

    def visit(block, carry):
        block_first = first_page + block * BLOCK_PAGES
        logical = block_first + jnp.arange(BLOCK_PAGES)
        physical = lax.dynamic_slice(table_row, (block_first,), (BLOCK_PAGES,))
        slots = jnp.clip(physical - offset, 0, pages_local - 1)
        block_keys = k_cache[slots].reshape(block_rows, local_heads, HD)
        block_values = v_cache[slots].reshape(block_rows, local_heads, HD)
        key_places = (logical[:, None] * page_rows + jnp.arange(page_rows)[None, :]).reshape(
            block_rows
        )
        usable = jnp.repeat(logical < last_page, page_rows) & (key_places < length)
        allowed = jnp.broadcast_to(usable[None, :], (all_rows, block_rows))
        return absorb(carry, queries, block_keys, block_values, allowed, scale)

    running_max, running_sum, output = lax.fori_loop(0, block_count, visit, state)
    peer_start = (1 - parity) * own_rows
    own_start = parity * own_rows
    outgoing = (
        lax.dynamic_slice_in_dim(output, peer_start, own_rows, 0),
        lax.dynamic_slice_in_dim(running_max, peer_start, own_rows, 2),
        lax.dynamic_slice_in_dim(running_sum, peer_start, own_rows, 2),
    )
    other_output, other_max, other_sum = (
        from_partner(outgoing[0].astype(jnp.bfloat16), "req", 0).astype(jnp.float32),
        from_partner(outgoing[1].astype(jnp.bfloat16), "req", 0).astype(jnp.float32),
        from_partner(outgoing[2].astype(jnp.bfloat16), "req", 0).astype(jnp.float32),
    )
    mine_output = lax.dynamic_slice_in_dim(output, own_start, own_rows, 0)
    mine_max = lax.dynamic_slice_in_dim(running_max, own_start, own_rows, 2)
    mine_sum = lax.dynamic_slice_in_dim(running_sum, own_start, own_rows, 2)
    joint_max = jnp.maximum(mine_max, other_max)
    mine_factor = jnp.exp(mine_max - joint_max)
    other_factor = jnp.exp(other_max - joint_max)
    joint_sum = mine_sum * mine_factor + other_sum * other_factor
    joint_output = (
        mine_output * jnp.transpose(mine_factor, (2, 0, 1))[..., None]
        + other_output * jnp.transpose(other_factor, (2, 0, 1))[..., None]
    )
    attention = (
        (joint_output / jnp.transpose(joint_sum, (2, 0, 1))[..., None])
        .reshape(own_rows, local_heads * GROUP * HD)
        .astype(jnp.bfloat16)
    )
    partial_value = lax.dot_general(
        lax.all_gather(attention, "req", axis=0, tiled=True),
        w_out,
        (((1,), (1,)), ((), ())),
        preferred_element_type=jnp.float32,
    )
    return lax.all_to_all(
        tensor_total(partial_value), "req", split_axis=0, concat_axis=1, tiled=True
    )


def solution(mesh):
    in_specs = (
        P("req", "tp"),
        P("req", "tp"),
        P("req", "tp"),
        P("req", None, "tp"),
        P("req", None, "tp"),
        P(),
        P(),
        P("req", "tp"),
    )
    out_specs = P("req", None)
    return jax.shard_map(shards, mesh=mesh, in_specs=in_specs, out_specs=out_specs, check_vma=False)
```

profile of v0, /device:TPU:1, one launch (start us, length us, event | category | flops | bytes accessed | tf_op | source)
XLA Modules:
  0.0 280.3 jit_solution(12929491694747640108)
XLA Ops:
  6.5 8.9 %collective-permute-start.2 = (bf16[64,1,128]{2,0,1:T(8,128)(2,1)}, bf16[64,1,128]{2,0,1:T(8,128)(2,1)S(1)}, u32[]{:S(2)}, u32[]{:S(2)}) collective-permute-start(bf16[64,1,128]{2,0,1:T(8,128)(2,1)} %bitcast.155), channel_id=1, source_target_pairs={{0,8},{8,0},{16,24},{24,16},{32,40},{40,32},{48,56},{56,48},{64,72... | collective-permute-start | bytes 49160 | tf_op jit(solution)/shard_map/ppermute | solution.py:15
  15.5 1.3 dynamic_slice.27
  17.4 0.7 convert_bitcast_fusion
  18.4 0.8 fusion.34
  19.3 1.9 collective-permute-start
  21.2 1.0 reshape.300
  22.5 2.4 collective-permute-start.1
  27.2 21.1 %while.14 = (s32[]{:T(128)}, f32[1,5,128]{2,1,0:T(8,128)S(1)}, f32[1,5,128]{2,1,0:T(8,128)S(1)}, f32[128,1,5,128]{0,3,2,1:T(8,128)S(1)}, s32[]{:T(128)}, /*index...) while((s32[]{:T(128)}, f32[1,5,128]{2,1,0:T(8,128)S(1)}, ...), condition=%wide.region_5.6_spmd, body=%wide.region_2.5_spmd.sunk | while | flops 170889632 | bytes 5585255 | solution.py:118
  27.4 0.7 fusion.81
  28.1 1.6 gather_fusion.1
  29.7 1.6 gather_fusion
  32.6 0.7 fusion.81
  33.3 1.6 gather_fusion.1
  35.0 1.6 gather_fusion
  37.9 0.7 fusion.81
  38.6 1.6 gather_fusion.1
  40.2 1.6 gather_fusion
  43.2 0.7 fusion.81
  43.9 1.6 gather_fusion.1
  45.5 1.6 gather_fusion
  48.5 1.9 collective-permute-start.5
  50.4 2.4 collective-permute-start.3
  52.9 1.9 collective-permute-start.4
  54.9 1.3 collective-permute-done.4
  56.4 0.8 copy.51
  57.2 85.2 %all-gather.2.cloned.1.call-done = bf16[4096,640]{1,0:T(8,128)(2,1)} async-done(((bf16[64,640]{1,0:T(8,128)(2,1)}), bf16[4096,640]{1,0:T(8,128)(2,1)}) %all-gather.2.cloned.1.call-update) | async-done | bytes 5242896 | tf_op jit(solution)/shard_map/all_gather | solution.py:148
  142.4 4.2 %convolution_convert_fusion = bf16[4096,80]{0,1:T(8,128)(2,1)S(1)} fusion(bf16[4096,640]{1,0:T(8,128)(2,1)} %all-gather.2.cloned.1.call-done, bf16[80,640]{1,0:T(8,128)(2,1)S(1)} %copy-done), kind=kOutput, calls=%fused_computation.31 | convolution fusion | flops 419758080 | bytes 6000640 | tf_op jit(solution)/shard_map/dot_general | solution.py:147
  146.6 2.5 all_to_all.14
  149.1 75.8 %all-reduce.3.cloned.1.call-done = bf16[64,64,80]{1,0,2:T(8,128)(2,1)} async-done(((bf16[64,64,80]{1,0,2:T(8,128)(2,1)}), bf16[64,64,80]{1,0,2:T(8,128)(2,1)}) %all-reduce.3.cloned.1.call-update) | async-done | bytes 655376 | tf_op jit(solution)/shard_map/psum | solution.py:51
  224.9 2.5 copy.43
  227.4 42.4 %all_to_all.19 = bf16[64,64,80]{2,1,0:T(8,128)(2,1)S(1)} all-to-all(bf16[64,64,80]{2,1,0:T(8,128)(2,1)S(1)} %copy.43), channel_id=1, replica_groups=mesh['req'=64,'tp'=8] {'req'}, dimensions={0} | all-to-all | bytes 1310720 | tf_op jit(solution)/shard_map/all_to_all | solution.py:153
  270.5 3.0 %all_to_all.17 = bf16[64,5120]{1,0:T(8,128)(2,1)} reshape(bf16[64,64,80]{2,1,0:T(8,128)(2,1)S(1)} %copy.44) | data formatting | bytes 1310720 | tf_op jit(solution)/shard_map/all_to_all | solution.py:153
  (76 shorter events, 8.3 us)
Async XLA Ops:
  6.5 135.9 %copy-start = (bf16[80,640]{1,0:T(8,128)(2,1)S(1)}, bf16[80,640]{1,0:T(8,128)(2,1)}, u32[]{:S(2)}) copy-start(bf16[80,640]{1,0:T(8,128)(2,1)} %param.17) | copy-start | bytes 307204
  6.5 135.9 %all-gather.2.cloned.1.call-start = ((), (), s32[]{:S(2)}) async-start(), calls=%async_computation.1 | async-start | bytes 5324800 | tf_op jit(solution)/shard_map/all_gather | solution.py:148
  6.5 20.4 %collective-permute-start.2 = (bf16[64,1,128]{2,0,1:T(8,128)(2,1)}, bf16[64,1,128]{2,0,1:T(8,128)(2,1)S(1)}, u32[]{:S(2)}, u32[]{:S(2)}) collective-permute-start(bf16[64,1,128]{2,0,1:T(8,128)(2,1)} %bitcast.155), channel_id=1, source_target_pairs={{0,8},{8,0},{16,24},{24,16},{32,40},{40,32},{48,56},{56,48},{64,72... | collective-permute-start | bytes 49160 | tf_op jit(solution)/shard_map/ppermute | solution.py:15
  19.3 7.2 %collective-permute-start = (bf16[64,1,128]{2,0,1:T(8,128)(2,1)S(1)}, bf16[64,1,128]{2,0,1:T(8,128)(2,1)S(1)}, u32[]{:S(2)}, u32[]{:S(2)}) collective-permute-start(bf16[64,1,128]{2,0,1:T(8,128)(2,1)S(1)} %bitcast.154), channel_id=1, source_target_pairs={{0,8},{8,0},{16,24},{24,16},{32,40},{40,32},{48,56},{56,48},{64,72... | collective-permute-start | bytes 49160 | tf_op jit(solution)/shard_map/ppermute | solution.py:15
  22.5 3.9 %collective-permute-start.1 = (bf16[64,5,128]{2,1,0:T(8,128)(2,1)S(1)}, bf16[64,5,128]{2,1,0:T(8,128)(2,1)S(1)}, u32[]{:S(2)}, u32[]{:S(2)}) collective-permute-start(bf16[64,5,128]{2,1,0:T(8,128)(2,1)S(1)} %fusion.25), channel_id=1, source_target_pairs={{0,8},{8,0},{16,24},{24,16},{32,40},{40,32},{48,56},{56,48},{64,72... | collective-permute-start | bytes 245768 | tf_op jit(solution)/shard_map/ppermute | solution.py:15
  25.5 1.4 copy-start.1
  48.5 6.4 %collective-permute-start.5 = (bf16[1,5,64]{2,1,0:T(8,128)(2,1)S(1)}, bf16[1,5,64]{2,1,0:T(8,128)(2,1)S(1)}, u32[]{:S(2)}, u32[]{:S(2)}) collective-permute-start(bf16[1,5,64]{2,1,0:T(8,128)(2,1)S(1)} %dynamic-slice_convert_fusion.1), channel_id=1, source_target_pairs={{0,8},{8,0},{16,24},{24,16},{32,40},{40,32},{48,56},{56,48},{64,72... | collective-permute-start | bytes 1928 | tf_op jit(solution)/shard_map/ppermute | solution.py:15
  50.4 4.5 %collective-permute-start.3 = (bf16[1,5,64]{2,1,0:T(8,128)(2,1)S(1)}, bf16[1,5,64]{2,1,0:T(8,128)(2,1)S(1)}, u32[]{:S(2)}, u32[]{:S(2)}) collective-permute-start(bf16[1,5,64]{2,1,0:T(8,128)(2,1)S(1)} %dynamic-slice_convert_fusion.2), channel_id=1, source_target_pairs={{0,8},{8,0},{16,24},{24,16},{32,40},{40,32},{48,56},{56,48},{64,72... | collective-permute-start | bytes 1928 | tf_op jit(solution)/shard_map/ppermute | solution.py:15
  52.9 3.3 %collective-permute-start.4 = (bf16[64,1,5,128]{0,3,2,1:T(8,128)(2,1)S(1)}, bf16[64,1,5,128]{0,3,2,1:T(8,128)(2,1)S(1)}, u32[]{:S(2)}, u32[]{:S(2)}) collective-permute-start(bf16[64,1,5,128]{0,3,2,1:T(8,128)(2,1)S(1)} %dynamic-slice_convert_fusion), channel_id=1, source_target_pairs={{0,8},{8,0},{16,24},{24,16},{32,40},{40,32},{48,56},{56,48},{64,72... | collective-permute-start | bytes 245768 | tf_op jit(solution)/shard_map/ppermute | solution.py:15
  57.2 167.7 %all-reduce.3.cloned.1.call-start = ((), (), s32[]{:S(2)}) async-start(), calls=%async_computation.2 | async-start | bytes 2621440 | tf_op jit(solution)/shard_map/psum | solution.py:51
Sparse Core Ops, SparseCore 0:
  57.3 85.0 all-gather.1
  149.2 75.6 all-reduce.2
where the time goes:
time: 281 us; the launch traced here: 280 us
  waiting for transfers between devices  162 us (58%)
  blocking collectives  42.4 us (15%)
  local copies, waits for them, and re-layouts  25.5 us (9%)
  starting transfers between devices  19.5 us (7%)
  between operations  15 us (5%)
  matrix products  8.07 us (3%)
  other arithmetic  7.05 us (3%)
    all_gather x1, waiting for transfers between devices, shards(): lax.all_gather(attention, 'req', axis=0, tiled=True)  85.2 us
    psum x1, waiting for transfers between devices, tensor_total(): return lax.psum(partial_value.astype(jnp.bfloat16), 'tp')  75.8 us
    all_to_all x1, blocking collectives, shards(): lax.all_to_all(tensor_total(partial_value), 'req', split_axis=0, concat_a...  42.4 us
    ppermute x6, starting transfers between devices, from_partner(): lax.ppermute(value, axis, [(i, i ^ 1 << distance) for i in range(lax.axis...  19.5 us
    gather x4, local copies, waits for them, and re-layouts, visit(): block_values = v_cache[slots].reshape(block_rows, local_heads, HD)  6.46 us
    gather x4, local copies, waits for them, and re-layouts, visit(): block_keys = k_cache[slots].reshape(block_rows, local_heads, HD)  6.46 us
    all_to_all x3, local copies, waits for them, and re-layouts, shards(): lax.all_to_all(tensor_total(partial_value), 'req', split_axis=0, concat_a...  6.1 us
  transfers between devices with their start and end apart: 8, of which 3 were waited for; matrix products, arithmetic and copies ran while one was open for 2% of the time, Pallas kernels for 0%

commit v1 on v0

--- a/solution.py
+++ b/solution.py
@@ -145,7 +145,9 @@
         .astype(jnp.bfloat16)
     )
     partial_value = lax.dot_general(
-        lax.all_gather(attention, "req", axis=0, tiled=True),
+        jnp.concatenate(
+            lax.all_to_all(jnp.stack([attention] * lax.axis_size("req")), "req", 0, 0), axis=0
+        ),
         w_out,
         (((1,), (1,)), ((), ())),
         preferred_element_type=jnp.float32,

time: 281 us -> 320 us (1.14)
  blocking collectives: 42.4 us -> 168 us
  waiting for transfers between devices: 162 us -> 77.8 us
    all_to_all x0 -> x1, blocking collectives: none -> 126 us  [shards(): lax.all_to_all(jnp.stack([attention] * lax.axis_size('req')), 'req', 0, 0)]
    all_gather x1 -> x0, waiting for transfers between devices: 85.2 us -> none  [shards(): lax.all_gather(attention, 'req', axis=0, tiled=True)]
  transfers between devices with their start and end apart: 8 -> 7, of which waited for: 3 -> 2; matrix products, arithmetic and copies ran while one was open for 2% -> 2% of each run, Pallas kernels for 0% -> 0%
where the time goes in v1:
time: 320 us; the launch traced here: 319 us
  blocking collectives  168 us (52%)
  waiting for transfers between devices  77.8 us (24%)
  local copies, waits for them, and re-layouts  25.6 us (8%)
  starting transfers between devices  19.5 us (6%)
  between operations  14.9 us (5%)
  other arithmetic  6.75 us (2%)
  matrix products  5.6 us (2%)
    all_to_all x1, blocking collectives, shards(): lax.all_to_all(jnp.stack([attention] * lax.axis_size('req')), 'req', 0, 0)  126 us
    psum x1, waiting for transfers between devices, tensor_total(): return lax.psum(partial_value.astype(jnp.bfloat16), 'tp')  76.5 us
    all_to_all x1, blocking collectives, shards(): lax.all_to_all(tensor_total(partial_value), 'req', split_axis=0, concat_a...  42.4 us
    ppermute x6, starting transfers between devices, from_partner(): lax.ppermute(value, axis, [(i, i ^ 1 << distance) for i in range(lax.axis...  19.5 us
    gather x4, local copies, waits for them, and re-layouts, visit(): block_keys = k_cache[slots].reshape(block_rows, local_heads, HD)  6.46 us
    gather x4, local copies, waits for them, and re-layouts, visit(): block_values = v_cache[slots].reshape(block_rows, local_heads, HD)  6.46 us
  transfers between devices with their start and end apart: 7, of which 2 were waited for; matrix products, arithmetic and copies ran while one was open for 2% of the time, Pallas kernels for 0%

profile of v1, /device:TPU:1, one launch (start us, length us, event | category | flops | bytes accessed | tf_op | source)
XLA Modules:
  0.0 318.6 jit_solution(14363549617257934311)
XLA Ops:
  6.5 8.9 %collective-permute-start.2 = (bf16[64,1,128]{2,0,1:T(8,128)(2,1)}, bf16[64,1,128]{2,0,1:T(8,128)(2,1)S(1)}, u32[]{:S(2)}, u32[]{:S(2)}) collective-permute-start(bf16[64,1,128]{2,0,1:T(8,128)(2,1)} %bitcast.157), channel_id=1, source_target_pairs={{0,8},{8,0},{16,24},{24,16},{32,40},{40,32},{48,56},{56,48},{64,72... | collective-permute-start | bytes 49160 | tf_op jit(solution)/shard_map/ppermute | solution.py:15
  15.5 1.2 dynamic_slice.27
  17.3 0.7 convert_bitcast_fusion
  18.3 0.8 fusion.34
  19.1 1.9 collective-permute-start
  21.1 1.0 reshape.307
  22.4 2.4 collective-permute-start.1
  25.4 0.7 fusion.57
  27.0 20.8 %while.14 = (s32[]{:T(128)}, f32[1,5,128]{2,1,0:T(8,128)S(1)}, f32[1,5,128]{2,1,0:T(8,128)S(1)}, f32[128,1,5,128]{0,3,2,1:T(8,128)S(1)}, s32[]{:T(128)}, /*index...) while((s32[]{:T(128)}, f32[1,5,128]{2,1,0:T(8,128)S(1)}, ...), condition=%wide.region_5.6_spmd, body=%wide.region_2.5_spmd.sunk | while | flops 170889632 | bytes 5585255 | solution.py:118
  27.8 1.6 gather_fusion.1
  29.4 1.6 gather_fusion
  32.4 0.6 fusion.81
  33.0 1.6 gather_fusion.1
  34.6 1.6 gather_fusion
  38.2 1.6 gather_fusion.1
  39.8 1.6 gather_fusion
  42.8 0.6 fusion.81
  43.4 1.6 gather_fusion.1
  45.0 1.6 gather_fusion
  48.0 1.9 collective-permute-start.5
  49.9 2.4 collective-permute-start.3
  52.4 1.9 collective-permute-start.4
  54.5 1.3 collective-permute-done.4
  56.0 0.8 stack.2
  56.8 125.7 %all_to_all.24 = bf16[64,64,640]{2,1,0:T(8,128)(2,1)S(1)} all-to-all(bf16[64,64,640]{2,1,0:T(8,128)(2,1)S(1)} %stack.2), channel_id=1, replica_groups=mesh['req'=64,'tp'=8] {'req'}, dimensions={0} | all-to-all | bytes 10485760 | tf_op jit(solution)/shard_map/all_to_all | solution.py:149
  182.5 1.7 convolution_convert_fusion
  184.2 2.5 all_to_all.18
  186.7 76.5 %all-reduce.3.cloned.1.call-done = bf16[64,64,80]{1,0,2:T(8,128)(2,1)} async-done(((bf16[64,64,80]{1,0,2:T(8,128)(2,1)}), bf16[64,64,80]{1,0,2:T(8,128)(2,1)}) %all-reduce.3.cloned.1.call-update) | async-done | bytes 655376 | tf_op jit(solution)/shard_map/psum | solution.py:51
  263.2 2.5 copy.37
  265.7 42.4 %all_to_all.25 = bf16[64,64,80]{2,1,0:T(8,128)(2,1)S(1)} all-to-all(bf16[64,64,80]{2,1,0:T(8,128)(2,1)S(1)} %copy.37), channel_id=1, replica_groups=mesh['req'=64,'tp'=8] {'req'}, dimensions={0} | all-to-all | bytes 1310720 | tf_op jit(solution)/shard_map/all_to_all | solution.py:155
  308.1 0.7 copy.38
  308.7 3.0 all_to_all.21
  (75 shorter events, 8.3 us)
Async XLA Ops:
  6.5 175.9 %copy-start = (bf16[80,640]{1,0:T(8,128)(2,1)S(1)}, bf16[80,640]{1,0:T(8,128)(2,1)}, u32[]{:S(2)}) copy-start(bf16[80,640]{1,0:T(8,128)(2,1)} %param.17) | copy-start | bytes 307204
  6.5 256.6 %all-reduce.3.cloned.1.call-start = ((), (), s32[]{:S(2)}) async-start(), calls=%async_computation.2 | async-start | bytes 2621440 | tf_op jit(solution)/shard_map/psum | solution.py:51
  6.5 20.3 %collective-permute-start.2 = (bf16[64,1,128]{2,0,1:T(8,128)(2,1)}, bf16[64,1,128]{2,0,1:T(8,128)(2,1)S(1)}, u32[]{:S(2)}, u32[]{:S(2)}) collective-permute-start(bf16[64,1,128]{2,0,1:T(8,128)(2,1)} %bitcast.157), channel_id=1, source_target_pairs={{0,8},{8,0},{16,24},{24,16},{32,40},{40,32},{48,56},{56,48},{64,72... | collective-permute-start | bytes 49160 | tf_op jit(solution)/shard_map/ppermute | solution.py:15
  19.1 7.1 %collective-permute-start = (bf16[64,1,128]{2,0,1:T(8,128)(2,1)S(1)}, bf16[64,1,128]{2,0,1:T(8,128)(2,1)S(1)}, u32[]{:S(2)}, u32[]{:S(2)}) collective-permute-start(bf16[64,1,128]{2,0,1:T(8,128)(2,1)S(1)} %bitcast.156), channel_id=1, source_target_pairs={{0,8},{8,0},{16,24},{24,16},{32,40},{40,32},{48,56},{56,48},{64,72... | collective-permute-start | bytes 49160 | tf_op jit(solution)/shard_map/ppermute | solution.py:15
  22.4 3.8 %collective-permute-start.1 = (bf16[64,5,128]{2,1,0:T(8,128)(2,1)S(1)}, bf16[64,5,128]{2,1,0:T(8,128)(2,1)S(1)}, u32[]{:S(2)}, u32[]{:S(2)}) collective-permute-start(bf16[64,5,128]{2,1,0:T(8,128)(2,1)S(1)} %fusion.25), channel_id=1, source_target_pairs={{0,8},{8,0},{16,24},{24,16},{32,40},{40,32},{48,56},{56,48},{64,72... | collective-permute-start | bytes 245768 | tf_op jit(solution)/shard_map/ppermute | solution.py:15
  25.4 1.5 copy-start.1
  48.0 6.4 %collective-permute-start.5 = (bf16[1,5,64]{2,1,0:T(8,128)(2,1)S(1)}, bf16[1,5,64]{2,1,0:T(8,128)(2,1)S(1)}, u32[]{:S(2)}, u32[]{:S(2)}) collective-permute-start(bf16[1,5,64]{2,1,0:T(8,128)(2,1)S(1)} %dynamic-slice_convert_fusion.1), channel_id=1, source_target_pairs={{0,8},{8,0},{16,24},{24,16},{32,40},{40,32},{48,56},{56,48},{64,72... | collective-permute-start | bytes 1928 | tf_op jit(solution)/shard_map/ppermute | solution.py:15
  49.9 4.5 %collective-permute-start.3 = (bf16[1,5,64]{2,1,0:T(8,128)(2,1)S(1)}, bf16[1,5,64]{2,1,0:T(8,128)(2,1)S(1)}, u32[]{:S(2)}, u32[]{:S(2)}) collective-permute-start(bf16[1,5,64]{2,1,0:T(8,128)(2,1)S(1)} %dynamic-slice_convert_fusion.2), channel_id=1, source_target_pairs={{0,8},{8,0},{16,24},{24,16},{32,40},{40,32},{48,56},{56,48},{64,72... | collective-permute-start | bytes 1928 | tf_op jit(solution)/shard_map/ppermute | solution.py:15
  52.4 3.3 %collective-permute-start.4 = (bf16[64,1,5,128]{0,3,2,1:T(8,128)(2,1)S(1)}, bf16[64,1,5,128]{0,3,2,1:T(8,128)(2,1)S(1)}, u32[]{:S(2)}, u32[]{:S(2)}) collective-permute-start(bf16[64,1,5,128]{0,3,2,1:T(8,128)(2,1)S(1)} %dynamic-slice_convert_fusion), channel_id=1, source_target_pairs={{0,8},{8,0},{16,24},{24,16},{32,40},{40,32},{48,56},{56,48},{64,72... | collective-permute-start | bytes 245768 | tf_op jit(solution)/shard_map/ppermute | solution.py:15
Sparse Core Ops, SparseCore 0:
  186.8 76.3 all-reduce.2
